TPU v7x, 256 devices: a whole 4x4x8 slice. The times are simulated.
256 devices in a mesh: rad: 16 (over x, y_hi, core), azi: 16 (over z, y_lo).
Axes of the slice: x: 4, y: 4 (y_hi: 2, y_lo: 2; y = y_hi * 2 + y_lo), z: 8, core: 2. Of those that a mesh axis runs over, the one named last changes fastest.
Arguments:
- fields: float32 [5, 512, 256, 128], P(None, 'rad', 'azi'), may hold values from -6 to 6
- kappa: float32 [512, 256, 128], P('rad', 'azi'), may hold values from 0.01 to 0.1
- radial_speed: float32 [5, 512], P(None, 'rad'), may hold values from -0.5 to 0.5
- azimuth_speed: float32 [5, 512], P(None, 'rad'), may hold values from -0.5 to 0.5
- shifts: int32 [512], P('rad'), may hold values from 0 to 255
Outputs:
- advanced: float32 [5, 512, 256, 128], P(None, 'rad', 'azi')
All inputs are finite; a program needn't handle non-finite values.
Results may differ from a plain program's by a relative error of at most 0.00002.
Values sent between devices are 32-bit elements; how exact they have to be, the bound alone decides.
No kernel may reach another device: no remote copies, remote signals or barrier semaphores. Data moves between devices by JAX's collectives and lax.ppermute only.
A program may use at most 64 MiB of HBM per device.

v0:
```python
import jax
import jax.numpy as jnp
from jax import lax
from jax.sharding import PartitionSpec as P


def stencil(padded, kap, speed_r, speed_p):
    n_r = padded.shape[1] - 4
    n_p = padded.shape[2] - 4

    def tap(a, b):
        return padded[:, 2 + a : 2 + a + n_r, 2 + b : 2 + b + n_p, :]

    centre = tap(0, 0)
    height = centre.shape[3]
    zpad = jnp.pad(centre, ((0, 0), (0, 0), (0, 0), (2, 2)))

    def ztap(a):
        return zpad[:, :, :, 2 + a : 2 + a + height]

    first_r = (tap(-2, 0) - 8.0 * tap(-1, 0) + 8.0 * tap(1, 0) - tap(2, 0)) / 12.0
    first_p = (tap(0, -2) - 8.0 * tap(0, -1) + 8.0 * tap(0, 1) - tap(0, 2)) / 12.0
    second_r = (
        -tap(-2, 0) + 16.0 * tap(-1, 0) - 30.0 * centre + 16.0 * tap(1, 0) - tap(2, 0)
    ) / 12.0
    second_p = (
        -tap(0, -2) + 16.0 * tap(0, -1) - 30.0 * centre + 16.0 * tap(0, 1) - tap(0, 2)
    ) / 12.0
    second_z = (-ztap(-2) + 16.0 * ztap(-1) - 30.0 * centre + 16.0 * ztap(1) - ztap(2)) / 12.0
    return (
        -speed_r[:, :, None, None] * first_r
        - speed_p[:, :, None, None] * first_p
        + kap[None] * (second_r + second_p + second_z)
    )


def extend(cells, width):
    sectors, rings = (lax.axis_size("azi"), lax.axis_size("rad"))
    rows, cols = (cells.shape[-3], cells.shape[-2])
    left = lax.ppermute(
        cells[..., cols - width :, :], "azi", [(i, (i + 1) % sectors) for i in range(sectors)]
    )
    right = lax.ppermute(
        cells[..., :width, :], "azi", [((i + 1) % sectors, i) for i in range(sectors)]
    )
    above = lax.ppermute(
        cells[..., rows - width :, :, :], "rad", [(i, i + 1) for i in range(rings - 1)]
    )
    below = lax.ppermute(cells[..., :width, :, :], "rad", [(i + 1, i) for i in range(rings - 1)])
    wide = jnp.concatenate([left, cells, right], axis=-2)
    corners = [(0, 0)] * (cells.ndim - 2) + [(width, width), (0, 0)]
    return jnp.concatenate([jnp.pad(above, corners), wide, jnp.pad(below, corners)], axis=-3)


def heun_sections(field, kappa, speed_r, speed_p):
    first = field + stencil(extend(field, 2), kappa, speed_r, speed_p)
    return 0.5 * (field + first + stencil(extend(first, 2), kappa, speed_r, speed_p))


def shift_rows(half, shifts):
    peers = lax.axis_size("azi")
    rows = half.shape[1]
    per = rows // peers
    full = lax.all_to_all(half, "azi", 1, 2, tiled=True)
    length = full.shape[2]
    first = lax.axis_index("azi") * per
    mine = lax.dynamic_slice_in_dim(shifts, first, per)
    doubled = jnp.concatenate([full, full], axis=2)
    rolled = []
    for row in range(per):
        start = (length - mine[row] % length) % length
        rolled.append(lax.dynamic_slice_in_dim(doubled[:, row], start, length, axis=1))
    moved = jnp.stack(rolled, axis=1)
    return lax.all_to_all(moved, "azi", 2, 1, tiled=True)


def shards(fields, kappa, radial_speed, azimuth_speed, shifts):
    fcount = fields.shape[0]
    bounds = [0, (fcount + 1) // 2, fcount]
    groups = [
        (fields[lo:hi], radial_speed[lo:hi], azimuth_speed[lo:hi])
        for lo, hi in zip(bounds, bounds[1:])
    ]
    halves = [heun_sections(f, kappa, r, p) for f, r, p in groups]
    moved = [shift_rows(h, shifts) for h in halves]
    done = [heun_sections(m, kappa, r, p) for m, (_, r, p) in zip(moved, groups)]
    return jnp.concatenate(done, axis=0)


def solution(mesh):
    placed = (
        P(None, "rad", "azi", None),
        P("rad", "azi", None),
        P(None, "rad"),
        P(None, "rad"),
        P("rad"),
    )
    return jax.shard_map(
        shards, mesh=mesh, in_specs=placed, out_specs=P(None, "rad", "azi", None), check_vma=False
    )
```

profile of v0, /device:TPU:17, one launch (start us, length us, event | category | flops | bytes accessed | tf_op | source)
XLA Modules:
  0.0 201.3 jit_solution(1181467208800410658)
XLA Ops:
  0.0 1.3 fusion.119
  1.3 1.1 collective-permute-start.1
  2.4 1.1 fusion.121
  3.5 1.9 collective-permute-start.17
  5.4 3.6 %collective-permute-start.18 = (f32[2,32,2,128]{3,2,1,0:T(2,128)S(1)}, f32[2,32,2,128]{3,2,1,0:T(2,128)S(1)}, u32[]{:S(2)}, u32[]{:S(2)}) collective-permute-start(f32[2,32,2,128]{3,2,1,0:T(2,128)S(1)} %get-tuple-element.12), channel_id=1, source_target_pairs={{1,0},{2,1},{3,2},{4,3},{5,4},{6,5},{7,6},{8,7},{9,8},{10,9},{11,1... | collective-permute-start | bytes 196616 | tf_op jit(solution)/shard_map/ppermute | solution.py:43
  8.9 0.8 fusion.120
  9.7 4.0 %collective-permute-start.16 = (f32[2,2,16,128]{3,2,1,0:T(8,128)S(1)}, f32[2,2,16,128]{3,2,1,0:T(8,128)S(1)}, u32[]{:S(2)}, u32[]{:S(2)}) collective-permute-start(f32[2,2,16,128]{3,2,1,0:T(8,128)S(1)} %get-tuple-element.9), channel_id=1, source_target_pairs={{0,16},{16,32},{32,48},{48,64},{64,80},{80,96},{96,112},{112,128},... | collective-permute-start | bytes 98312 | tf_op jit(solution)/shard_map/ppermute | solution.py:46
  13.7 1.9 collective-permute-start.19
  15.7 0.8 fusion.118
  16.5 1.0 broadcast_multiply_fusion
  17.7 2.4 %collective-permute-start.2 = (f32[3,32,2,128]{3,2,1,0:T(2,128)S(1)}, f32[3,32,2,128]{3,2,1,0:T(2,128)S(1)}, u32[]{:S(2)}, u32[]{:S(2)}) collective-permute-start(f32[3,32,2,128]{3,2,1,0:T(2,128)S(1)} %get-tuple-element.8), channel_id=1, source_target_pairs={{1,0},{2,1},{3,2},{4,3},{5,4},{6,5},{7,6},{8,7},{9,8},{10,9},{11,1... | collective-permute-start | bytes 294920 | tf_op jit(solution)/shard_map/ppermute | solution.py:43
  20.1 1.3 collective-permute-done.19
  21.4 4.4 %collective-permute-start = (f32[3,2,16,128]{3,2,1,0:T(8,128)S(1)}, f32[3,2,16,128]{3,2,1,0:T(8,128)S(1)}, u32[]{:S(2)}, u32[]{:S(2)}) collective-permute-start(f32[3,2,16,128]{3,2,1,0:T(8,128)S(1)} %get-tuple-element.5), channel_id=1, source_target_pairs={{0,16},{16,32},{32,48},{48,64},{64,80},{80,96},{96,112},{112,128},... | collective-permute-start | bytes 147464 | tf_op jit(solution)/shard_map/ppermute | solution.py:46
  25.8 1.9 collective-permute-start.3
  27.9 1.2 fusion.74
  29.2 0.4 collective-permute-start.21
  29.6 3.2 %collective-permute-start.22 = (f32[2,32,2,128]{3,2,1,0:T(2,128)S(1)}, f32[2,32,2,128]{3,2,1,0:T(2,128)S(1)}, u32[]{:S(2)}, u32[]{:S(2)}) collective-permute-start(f32[2,32,2,128]{3,2,1,0:T(2,128)S(1)} %get-tuple-element.56), channel_id=1, source_target_pairs={{1,0},{2,1},{3,2},{4,3},{5,4},{6,5},{7,6},{8,7},{9,8},{10,9},{11,1... | collective-permute-start | bytes 196616 | tf_op jit(solution)/shard_map/ppermute | solution.py:43
  32.9 0.8 collective-permute-done.3
  33.6 5.8 %collective-permute-start.20 = (f32[2,2,16,128]{3,2,1,0:T(8,128)S(1)}, f32[2,2,16,128]{3,2,1,0:T(8,128)S(1)}, u32[]{:S(2)}, u32[]{:S(2)}) collective-permute-start(f32[2,2,16,128]{3,2,1,0:T(8,128)S(1)} %get-tuple-element.53), channel_id=1, source_target_pairs={{0,16},{16,32},{32,48},{48,64},{64,80},{80,96},{96,112},{112,128},... | collective-permute-start | bytes 98312 | tf_op jit(solution)/shard_map/ppermute | solution.py:46
  39.5 1.9 collective-permute-start.23
  41.6 2.1 %fusion.16 = f32[3,32,16,128]{3,2,1,0:T(8,128)S(1)} fusion(f32[3,32,16,128]{3,2,1,0:T(8,128)S(1)} %slice.558, f32[3,32,2,128]{3,2,1,0:T(2,128)S(1)} %collective-permute-done.2, f32[3,32,2,128]{3,2,1,0:T(2,128)S(1)} %collective-permute-done.1, f32[3,34,20,128]{3,2,1,0:T(8,128)S(1)} %get-tuple-element.20, f32[3,34,20,128]{3,2,1,0:T(8,128)S(1)} %get-tuple-element.19, ...), kind=kLoop, calls=%fused_computation.89 | loop fusion | flops 8650752 | bytes 5178112 | tf_op jit(solution)/shard_map/add | solution.py:56
  43.9 3.6 %collective-permute-start.6 = (f32[3,32,2,128]{3,2,1,0:T(2,128)S(1)}, f32[3,32,2,128]{3,2,1,0:T(2,128)S(1)}, u32[]{:S(2)}, u32[]{:S(2)}) collective-permute-start(f32[3,32,2,128]{3,2,1,0:T(2,128)S(1)} %get-tuple-element.34), channel_id=1, source_target_pairs={{1,0},{2,1},{3,2},{4,3},{5,4},{6,5},{7,6},{8,7},{9,8},{10,9},{11,1... | collective-permute-start | bytes 294920 | tf_op jit(solution)/shard_map/ppermute | solution.py:43
  47.7 1.3 fusion.86
  49.0 0.9 copy.16
  49.8 5.5 %all-to-all-start.2 = ((f32[2,32,16,128]{3,2,0,1:T(8,128)}), f32[2,32,16,128]{3,2,0,1:T(8,128)S(1)}, u32[]{:S(2)}, u32[]{:S(2)}) async-start(f32[2,32,16,128]{3,2,0,1:T(8,128)} %copy.16), calls=%async_computation.2 | async-start | bytes 1048576 | tf_op jit(solution)/shard_map/all_to_all | solution.py:64
  55.3 6.9 %collective-permute-start.4 = (f32[3,2,16,128]{3,2,1,0:T(8,128)S(1)}, f32[3,2,16,128]{3,2,1,0:T(8,128)S(1)}, u32[]{:S(2)}, u32[]{:S(2)}) collective-permute-start(f32[3,2,16,128]{3,2,1,0:T(8,128)S(1)} %get-tuple-element.31), channel_id=1, source_target_pairs={{0,16},{16,32},{32,48},{48,64},{64,80},{80,96},{96,112},{112,128},... | collective-permute-start | bytes 147464 | tf_op jit(solution)/shard_map/ppermute | solution.py:46
  62.2 2.1 %collective-permute-start.7 = (f32[3,2,16,128]{3,2,1,0:T(8,128)S(1)}, f32[3,2,16,128]{3,2,1,0:T(8,128)S(1)}, u32[]{:S(2)}, u32[]{:S(2)}) collective-permute-start(f32[3,2,16,128]{3,2,1,0:T(8,128)S(1)} %get-tuple-element.32), channel_id=1, source_target_pairs={{16,0},{32,16},{48,32},{64,48},{80,64},{96,80},{112,96},{128,112},... | collective-permute-start | bytes 147464 | tf_op jit(solution)/shard_map/ppermute | solution.py:49
  64.3 6.0 %collective-permute-done.7 = f32[3,2,16,128]{3,2,1,0:T(8,128)S(1)} collective-permute-done((f32[3,2,16,128]{3,2,1,0:T(8,128)S(1)}, f32[3,2,16,128]{3,2,1,0:T(8,128)S(1)}, u32[]{:S(2)}, u32[]{:S(2)}) %collective-permute-start.7) | collective-permute-done | bytes 49184 | tf_op jit(solution)/shard_map/ppermute | solution.py:49
  70.6 2.1 %fusion.28 = f32[3,32,16,128]{3,2,1,0:T(8,128)S(1)} fusion(f32[3,32,16,128]{3,2,1,0:T(8,128)S(1)} %fusion.16, f32[3,32,2,128]{3,2,1,0:T(2,128)S(1)} %collective-permute-done.6, f32[3,32,2,128]{3,2,1,0:T(2,128)S(1)} %collective-permute-done.5, f32[3,34,20,128]{3,2,1,0:T(8,128)S(1)} %get-tuple-element.18, f32[3,34,20,128]{3,2,1,0:T(8,128)S(1)} %get-tuple-element.17, ...), kind=kLoop, calls=%fused_computation.101 | loop fusion | flops 9043968 | bytes 5964544 | tf_op jit(solution)/shard_map/mul | solution.py:57
  72.7 0.9 copy.10
  73.7 8.1 %all-to-all-start = ((f32[3,32,16,128]{3,2,0,1:T(8,128)}), f32[3,32,16,128]{3,2,0,1:T(8,128)S(1)}, u32[]{:S(2)}, u32[]{:S(2)}) async-start(f32[3,32,16,128]{3,2,0,1:T(8,128)} %copy.10), calls=%async_computation | async-start | bytes 1572864 | tf_op jit(solution)/shard_map/all_to_all | solution.py:64
  81.9 0.6 fusion.134
  86.6 1.2 copy.19
  87.8 14.5 %all-to-all-done = f32[3,32,16,128]{3,2,0,1:T(8,128)S(1)} async-done(((f32[3,32,16,128]{3,2,0,1:T(8,128)}), f32[3,32,16,128]{3,2,0,1:T(8,128)S(1)}, u32[]{:S(2)}, u32[]{:S(2)}) %all-to-all-start) | async-done | bytes 786464 | tf_op jit(solution)/shard_map/all_to_all | solution.py:64
  102.3 3.6 %all-to-all-start.3 = ((f32[2,2,256,128]{3,1,0,2:T(2,128)}), f32[2,2,256,128]{3,1,0,2:T(2,128)S(1)}, u32[]{:S(2)}, u32[]{:S(2)}) async-start(f32[2,2,256,128]{3,1,0,2:T(2,128)} %copy.19), calls=%async_computation.3 | async-start | bytes 1048576 | tf_op jit(solution)/shard_map/all_to_all | solution.py:74
  106.4 1.5 copy.13
  107.9 14.7 %all-to-all-done.3 = f32[2,2,256,128]{3,1,0,2:T(2,128)S(1)} async-done(((f32[2,2,256,128]{3,1,0,2:T(2,128)}), f32[2,2,256,128]{3,1,0,2:T(2,128)S(1)}, u32[]{:S(2)}, u32[]{:S(2)}) %all-to-all-start.3) | async-done | bytes 524320 | tf_op jit(solution)/shard_map/all_to_all | solution.py:74
  122.5 3.7 %all-to-all-start.1 = ((f32[3,2,256,128]{3,1,0,2:T(2,128)}), f32[3,2,256,128]{3,1,0,2:T(2,128)S(1)}, u32[]{:S(2)}, u32[]{:S(2)}) async-start(f32[3,2,256,128]{3,1,0,2:T(2,128)} %copy.13), calls=%async_computation.1 | async-start | bytes 1572864 | tf_op jit(solution)/shard_map/all_to_all | solution.py:74
  126.4 1.4 collective-permute-start.25
  127.8 2.2 %collective-permute-start.26 = (f32[2,32,2,128]{3,2,1,0:T(2,128)S(1)}, f32[2,32,2,128]{3,2,1,0:T(2,128)S(1)}, u32[]{:S(2)}, u32[]{:S(2)}) collective-permute-start(f32[2,32,2,128]{3,2,1,0:T(2,128)S(1)} %get-tuple-element.50), channel_id=1, source_target_pairs={{1,0},{2,1},{3,2},{4,3},{5,4},{6,5},{7,6},{8,7},{9,8},{10,9},{11,1... | collective-permute-start | bytes 196616 | tf_op jit(solution)/shard_map/ppermute | solution.py:43
  130.1 7.4 %collective-permute-start.24 = (f32[2,2,16,128]{3,2,1,0:T(8,128)S(1)}, f32[2,2,16,128]{3,2,1,0:T(8,128)S(1)}, u32[]{:S(2)}, u32[]{:S(2)}) collective-permute-start(f32[2,2,16,128]{3,2,1,0:T(8,128)S(1)} %get-tuple-element.47), channel_id=1, source_target_pairs={{0,16},{16,32},{32,48},{48,64},{64,80},{80,96},{96,112},{112,128},... | collective-permute-start | bytes 98312 | tf_op jit(solution)/shard_map/ppermute | solution.py:46
  137.5 1.9 collective-permute-start.27
  139.4 6.0 %collective-permute-done.27 = f32[2,2,16,128]{3,2,1,0:T(8,128)S(1)} collective-permute-done((f32[2,2,16,128]{3,2,1,0:T(8,128)S(1)}, f32[2,2,16,128]{3,2,1,0:T(8,128)S(1)}, u32[]{:S(2)}, u32[]{:S(2)}) %collective-permute-start.27) | collective-permute-done | bytes 32800 | tf_op jit(solution)/shard_map/ppermute | solution.py:49
  145.4 0.8 collective-permute-done.25
  146.4 1.2 fusion.97
  147.7 1.3 collective-permute-start.29
  149.0 2.3 %collective-permute-start.30 = (f32[2,32,2,128]{3,2,1,0:T(2,128)S(1)}, f32[2,32,2,128]{3,2,1,0:T(2,128)S(1)}, u32[]{:S(2)}, u32[]{:S(2)}) collective-permute-start(f32[2,32,2,128]{3,2,1,0:T(2,128)S(1)} %get-tuple-element.46), channel_id=1, source_target_pairs={{1,0},{2,1},{3,2},{4,3},{5,4},{6,5},{7,6},{8,7},{9,8},{10,9},{11,1... | collective-permute-start | bytes 196616 | tf_op jit(solution)/shard_map/ppermute | solution.py:43
  151.4 8.4 %collective-permute-start.28 = (f32[2,2,16,128]{3,2,1,0:T(8,128)S(1)}, f32[2,2,16,128]{3,2,1,0:T(8,128)S(1)}, u32[]{:S(2)}, u32[]{:S(2)}) collective-permute-start(f32[2,2,16,128]{3,2,1,0:T(8,128)S(1)} %get-tuple-element.43), channel_id=1, source_target_pairs={{0,16},{16,32},{32,48},{48,64},{64,80},{80,96},{96,112},{112,128},... | collective-permute-start | bytes 98312 | tf_op jit(solution)/shard_map/ppermute | solution.py:46
  159.8 1.9 collective-permute-start.31
  162.0 0.4 collective-permute-start.10
  162.4 1.1 collective-permute-start.9
  163.6 3.9 %collective-permute-done.31 = f32[2,2,16,128]{3,2,1,0:T(8,128)S(1)} collective-permute-done((f32[2,2,16,128]{3,2,1,0:T(8,128)S(1)}, f32[2,2,16,128]{3,2,1,0:T(8,128)S(1)}, u32[]{:S(2)}, u32[]{:S(2)}) %collective-permute-start.31) | collective-permute-done | bytes 32800 | tf_op jit(solution)/shard_map/ppermute | solution.py:49
  167.4 1.9 collective-permute-start.11
  169.4 6.3 %collective-permute-start.8 = (f32[3,2,16,128]{3,2,1,0:T(8,128)S(1)}, f32[3,2,16,128]{3,2,1,0:T(8,128)S(1)}, u32[]{:S(2)}, u32[]{:S(2)}) collective-permute-start(f32[3,2,16,128]{3,2,1,0:T(8,128)S(1)} %get-tuple-element.25), channel_id=1, source_target_pairs={{0,16},{16,32},{32,48},{48,64},{64,80},{80,96},{96,112},{112,128},... | collective-permute-start | bytes 147464 | tf_op jit(solution)/shard_map/ppermute | solution.py:46
  175.8 0.8 collective-permute-done.8
  176.6 0.2 select_maximum_fusion.3
  176.8 2.1 %fusion.39 = f32[3,32,16,128]{3,2,1,0:T(8,128)S(1)} fusion(f32[3,32,16,128]{3,2,1,0:T(8,128)S(1)} %bitcast.21, f32[3,32,2,128]{3,2,1,0:T(2,128)S(1)} %collective-permute-done.10, f32[3,32,2,128]{3,2,1,0:T(2,128)S(1)} %collective-permute-done.9, f32[3,34,20,128]{3,2,1,0:T(8,128)S(1)} %get-tuple-element.16, f32[3,34,20,128]{3,2,1,0:T(8,128)S(1)} %get-tuple-element.15, ...), kind=kLoop, calls=%fused_computation.112 | loop fusion | flops 8650752 | bytes 5178112 | tf_op jit(solution)/shard_map/add | solution.py:56
  179.1 3.6 %collective-permute-start.14 = (f32[3,32,2,128]{3,2,1,0:T(2,128)S(1)}, f32[3,32,2,128]{3,2,1,0:T(2,128)S(1)}, u32[]{:S(2)}, u32[]{:S(2)}) collective-permute-start(f32[3,32,2,128]{3,2,1,0:T(2,128)S(1)} %get-tuple-element.24), channel_id=1, source_target_pairs={{1,0},{2,1},{3,2},{4,3},{5,4},{6,5},{7,6},{8,7},{9,8},{10,9},{11,1... | collective-permute-start | bytes 294920 | tf_op jit(solution)/shard_map/ppermute | solution.py:43
  182.7 7.2 %collective-permute-start.12 = (f32[3,2,16,128]{3,2,1,0:T(8,128)S(1)}, f32[3,2,16,128]{3,2,1,0:T(8,128)S(1)}, u32[]{:S(2)}, u32[]{:S(2)}) collective-permute-start(f32[3,2,16,128]{3,2,1,0:T(8,128)S(1)} %get-tuple-element.21), channel_id=1, source_target_pairs={{0,16},{16,32},{32,48},{48,64},{64,80},{80,96},{96,112},{112,128},... | collective-permute-start | bytes 147464 | tf_op jit(solution)/shard_map/ppermute | solution.py:46
  189.9 1.9 collective-permute-start.15
  191.8 1.3 fusion.109
  193.1 4.6 %collective-permute-done.15 = f32[3,2,16,128]{3,2,1,0:T(8,128)S(1)} collective-permute-done((f32[3,2,16,128]{3,2,1,0:T(8,128)S(1)}, f32[3,2,16,128]{3,2,1,0:T(8,128)S(1)}, u32[]{:S(2)}, u32[]{:S(2)}) %collective-permute-start.15) | collective-permute-done | bytes 49184 | tf_op jit(solution)/shard_map/ppermute | solution.py:49
  197.9 2.2 %fusion.51 = f32[3,32,16,128]{3,2,1,0:T(8,128)S(1)} fusion(f32[3,32,16,128]{3,2,1,0:T(8,128)S(1)} %fusion.39, f32[3,32,2,128]{3,2,1,0:T(2,128)S(1)} %collective-permute-done.14, f32[3,32,2,128]{3,2,1,0:T(2,128)S(1)} %collective-permute-done.13, f32[3,34,20,128]{3,2,1,0:T(8,128)S(1)} %get-tuple-element.14, f32[3,34,20,128]{3,2,1,0:T(8,128)S(1)} %get-tuple-element.13, ...), kind=kLoop, calls=%fused_computation.124 | loop fusion | flops 9043968 | bytes 5964544 | tf_op jit(solution)/shard_map/mul | solution.py:57
  200.1 1.2 pad_maximum_fusion
  (74 shorter events, 3.1 us)
Async XLA Ops:
  0.0 17.5 %copy-start = (f32[5,32,16,128]{3,2,1,0:T(8,128)S(1)}, f32[5,32,16,128]{3,2,1,0:T(8,128)}, u32[]{:S(2)}) copy-start(f32[5,32,16,128]{3,2,1,0:T(8,128)} %param.5) | copy-start | bytes 3932164
  0.0 17.5 %copy-start.2 = (f32[5,32]{1,0:T(8,128)S(1)}, f32[5,32]{1,0:T(8,128)}, u32[]{:S(2)}) copy-start(f32[5,32]{1,0:T(8,128)} %param.7) | copy-start | bytes 1924
  0.0 17.5 %copy-start.1 = (f32[5,32]{1,0:T(8,128)S(1)}, f32[5,32]{1,0:T(8,128)}, u32[]{:S(2)}) copy-start(f32[5,32]{1,0:T(8,128)} %param.8) | copy-start | bytes 1924
  1.3 38.2 %collective-permute-start.1 = (f32[3,32,2,128]{3,2,1,0:T(2,128)S(1)}, f32[3,32,2,128]{3,2,1,0:T(2,128)S(1)}, u32[]{:S(2)}, u32[]{:S(2)}) collective-permute-start(f32[3,32,2,128]{3,2,1,0:T(2,128)S(1)} %get-tuple-element.7), channel_id=1, source_target_pairs={{0,1},{1,2},{2,3},{3,4},{4,5},{5,6},{6,7},{7,8},{8,9},{9,10},{10,1... | collective-permute-start | bytes 294920 | tf_op jit(solution)/shard_map/ppermute | solution.py:40
  3.5 22.3 %collective-permute-start.17 = (f32[2,32,2,128]{3,2,1,0:T(2,128)S(1)}, f32[2,32,2,128]{3,2,1,0:T(2,128)S(1)}, u32[]{:S(2)}, u32[]{:S(2)}) collective-permute-start(f32[2,32,2,128]{3,2,1,0:T(2,128)S(1)} %get-tuple-element.11), channel_id=1, source_target_pairs={{0,1},{1,2},{2,3},{3,4},{4,5},{5,6},{6,7},{7,8},{8,9},{9,10},{10,1... | collective-permute-start | bytes 196616 | tf_op jit(solution)/shard_map/ppermute | solution.py:40
  5.4 22.4 %collective-permute-start.18 = (f32[2,32,2,128]{3,2,1,0:T(2,128)S(1)}, f32[2,32,2,128]{3,2,1,0:T(2,128)S(1)}, u32[]{:S(2)}, u32[]{:S(2)}) collective-permute-start(f32[2,32,2,128]{3,2,1,0:T(2,128)S(1)} %get-tuple-element.12), channel_id=1, source_target_pairs={{1,0},{2,1},{3,2},{4,3},{5,4},{6,5},{7,6},{8,7},{9,8},{10,9},{11,1... | collective-permute-start | bytes 196616 | tf_op jit(solution)/shard_map/ppermute | solution.py:43
  9.7 7.9 %collective-permute-start.16 = (f32[2,2,16,128]{3,2,1,0:T(8,128)S(1)}, f32[2,2,16,128]{3,2,1,0:T(8,128)S(1)}, u32[]{:S(2)}, u32[]{:S(2)}) collective-permute-start(f32[2,2,16,128]{3,2,1,0:T(8,128)S(1)} %get-tuple-element.9), channel_id=1, source_target_pairs={{0,16},{16,32},{32,48},{48,64},{64,80},{80,96},{96,112},{112,128},... | collective-permute-start | bytes 98312 | tf_op jit(solution)/shard_map/ppermute | solution.py:46
  13.7 7.6 %collective-permute-start.19 = (f32[2,2,16,128]{3,2,1,0:T(8,128)S(1)}, f32[2,2,16,128]{3,2,1,0:T(8,128)S(1)}, u32[]{:S(2)}, u32[]{:S(2)}) collective-permute-start(f32[2,2,16,128]{3,2,1,0:T(8,128)S(1)} %get-tuple-element.10), channel_id=1, source_target_pairs={{16,0},{32,16},{48,32},{64,48},{80,64},{96,80},{112,96},{128,112},... | collective-permute-start | bytes 98312 | tf_op jit(solution)/shard_map/ppermute | solution.py:49
  17.7 23.7 %collective-permute-start.2 = (f32[3,32,2,128]{3,2,1,0:T(2,128)S(1)}, f32[3,32,2,128]{3,2,1,0:T(2,128)S(1)}, u32[]{:S(2)}, u32[]{:S(2)}) collective-permute-start(f32[3,32,2,128]{3,2,1,0:T(2,128)S(1)} %get-tuple-element.8), channel_id=1, source_target_pairs={{1,0},{2,1},{3,2},{4,3},{5,4},{6,5},{7,6},{8,7},{9,8},{10,9},{11,1... | collective-permute-start | bytes 294920 | tf_op jit(solution)/shard_map/ppermute | solution.py:43
  21.4 8.2 %collective-permute-start = (f32[3,2,16,128]{3,2,1,0:T(8,128)S(1)}, f32[3,2,16,128]{3,2,1,0:T(8,128)S(1)}, u32[]{:S(2)}, u32[]{:S(2)}) collective-permute-start(f32[3,2,16,128]{3,2,1,0:T(8,128)S(1)} %get-tuple-element.5), channel_id=1, source_target_pairs={{0,16},{16,32},{32,48},{48,64},{64,80},{80,96},{96,112},{112,128},... | collective-permute-start | bytes 147464 | tf_op jit(solution)/shard_map/ppermute | solution.py:46
  25.8 7.8 %collective-permute-start.3 = (f32[3,2,16,128]{3,2,1,0:T(8,128)S(1)}, f32[3,2,16,128]{3,2,1,0:T(8,128)S(1)}, u32[]{:S(2)}, u32[]{:S(2)}) collective-permute-start(f32[3,2,16,128]{3,2,1,0:T(8,128)S(1)} %get-tuple-element.6), channel_id=1, source_target_pairs={{16,0},{32,16},{48,32},{64,48},{80,64},{96,80},{112,96},{128,112},... | collective-permute-start | bytes 147464 | tf_op jit(solution)/shard_map/ppermute | solution.py:49
  29.2 18.3 %collective-permute-start.21 = (f32[2,32,2,128]{3,2,1,0:T(2,128)S(1)}, f32[2,32,2,128]{3,2,1,0:T(2,128)S(1)}, u32[]{:S(2)}, u32[]{:S(2)}) collective-permute-start(f32[2,32,2,128]{3,2,1,0:T(2,128)S(1)} %get-tuple-element.55), channel_id=1, source_target_pairs={{0,1},{1,2},{2,3},{3,4},{4,5},{5,6},{6,7},{7,8},{8,9},{9,10},{10,1... | collective-permute-start | bytes 196616 | tf_op jit(solution)/shard_map/ppermute | solution.py:40
  29.6 17.9 %collective-permute-start.22 = (f32[2,32,2,128]{3,2,1,0:T(2,128)S(1)}, f32[2,32,2,128]{3,2,1,0:T(2,128)S(1)}, u32[]{:S(2)}, u32[]{:S(2)}) collective-permute-start(f32[2,32,2,128]{3,2,1,0:T(2,128)S(1)} %get-tuple-element.56), channel_id=1, source_target_pairs={{1,0},{2,1},{3,2},{4,3},{5,4},{6,5},{7,6},{8,7},{9,8},{10,9},{11,1... | collective-permute-start | bytes 196616 | tf_op jit(solution)/shard_map/ppermute | solution.py:43
  33.6 10.3 %collective-permute-start.20 = (f32[2,2,16,128]{3,2,1,0:T(8,128)S(1)}, f32[2,2,16,128]{3,2,1,0:T(8,128)S(1)}, u32[]{:S(2)}, u32[]{:S(2)}) collective-permute-start(f32[2,2,16,128]{3,2,1,0:T(8,128)S(1)} %get-tuple-element.53), channel_id=1, source_target_pairs={{0,16},{16,32},{32,48},{48,64},{64,80},{80,96},{96,112},{112,128},... | collective-permute-start | bytes 98312 | tf_op jit(solution)/shard_map/ppermute | solution.py:46
  39.5 8.0 %collective-permute-start.23 = (f32[2,2,16,128]{3,2,1,0:T(8,128)S(1)}, f32[2,2,16,128]{3,2,1,0:T(8,128)S(1)}, u32[]{:S(2)}, u32[]{:S(2)}) collective-permute-start(f32[2,2,16,128]{3,2,1,0:T(8,128)S(1)} %get-tuple-element.54), channel_id=1, source_target_pairs={{16,0},{32,16},{48,32},{64,48},{80,64},{96,80},{112,96},{128,112},... | collective-permute-start | bytes 98312 | tf_op jit(solution)/shard_map/ppermute | solution.py:49
  43.8 26.5 %collective-permute-start.5 = (f32[3,32,2,128]{3,2,1,0:T(2,128)S(1)}, f32[3,32,2,128]{3,2,1,0:T(2,128)S(1)}, u32[]{:S(2)}, u32[]{:S(2)}) collective-permute-start(f32[3,32,2,128]{3,2,1,0:T(2,128)S(1)} %get-tuple-element.33), channel_id=1, source_target_pairs={{0,1},{1,2},{2,3},{3,4},{4,5},{5,6},{6,7},{7,8},{8,9},{9,10},{10,1... | collective-permute-start | bytes 294920 | tf_op jit(solution)/shard_map/ppermute | solution.py:40
  43.9 26.4 %collective-permute-start.6 = (f32[3,32,2,128]{3,2,1,0:T(2,128)S(1)}, f32[3,32,2,128]{3,2,1,0:T(2,128)S(1)}, u32[]{:S(2)}, u32[]{:S(2)}) collective-permute-start(f32[3,32,2,128]{3,2,1,0:T(2,128)S(1)} %get-tuple-element.34), channel_id=1, source_target_pairs={{1,0},{2,1},{3,2},{4,3},{5,4},{6,5},{7,6},{8,7},{9,8},{10,9},{11,1... | collective-permute-start | bytes 294920 | tf_op jit(solution)/shard_map/ppermute | solution.py:43
  49.8 23.8 %all-to-all-start.2 = ((f32[2,32,16,128]{3,2,0,1:T(8,128)}), f32[2,32,16,128]{3,2,0,1:T(8,128)S(1)}, u32[]{:S(2)}, u32[]{:S(2)}) async-start(f32[2,32,16,128]{3,2,0,1:T(8,128)} %copy.16), calls=%async_computation.2 | async-start | bytes 1048576 | tf_op jit(solution)/shard_map/all_to_all | solution.py:64
  55.3 9.0 %collective-permute-start.4 = (f32[3,2,16,128]{3,2,1,0:T(8,128)S(1)}, f32[3,2,16,128]{3,2,1,0:T(8,128)S(1)}, u32[]{:S(2)}, u32[]{:S(2)}) collective-permute-start(f32[3,2,16,128]{3,2,1,0:T(8,128)S(1)} %get-tuple-element.31), channel_id=1, source_target_pairs={{0,16},{16,32},{32,48},{48,64},{64,80},{80,96},{96,112},{112,128},... | collective-permute-start | bytes 147464 | tf_op jit(solution)/shard_map/ppermute | solution.py:46
  62.2 8.1 %collective-permute-start.7 = (f32[3,2,16,128]{3,2,1,0:T(8,128)S(1)}, f32[3,2,16,128]{3,2,1,0:T(8,128)S(1)}, u32[]{:S(2)}, u32[]{:S(2)}) collective-permute-start(f32[3,2,16,128]{3,2,1,0:T(8,128)S(1)} %get-tuple-element.32), channel_id=1, source_target_pairs={{16,0},{32,16},{48,32},{64,48},{80,64},{96,80},{112,96},{128,112},... | collective-permute-start | bytes 147464 | tf_op jit(solution)/shard_map/ppermute | solution.py:49
  72.7 9.1 %copy-start.3 = (s32[32]{0:T(128)S(1)}, s32[32]{0:T(128)}, u32[]{:S(2)}) copy-start(s32[32]{0:T(128)} %param.9) | copy-start | bytes 388
  73.7 28.7 %all-to-all-start = ((f32[3,32,16,128]{3,2,0,1:T(8,128)}), f32[3,32,16,128]{3,2,0,1:T(8,128)S(1)}, u32[]{:S(2)}, u32[]{:S(2)}) async-start(f32[3,32,16,128]{3,2,0,1:T(8,128)} %copy.10), calls=%async_computation | async-start | bytes 1572864 | tf_op jit(solution)/shard_map/all_to_all | solution.py:64
  102.3 20.2 %all-to-all-start.3 = ((f32[2,2,256,128]{3,1,0,2:T(2,128)}), f32[2,2,256,128]{3,1,0,2:T(2,128)S(1)}, u32[]{:S(2)}, u32[]{:S(2)}) async-start(f32[2,2,256,128]{3,1,0,2:T(2,128)} %copy.19), calls=%async_computation.3 | async-start | bytes 1048576 | tf_op jit(solution)/shard_map/all_to_all | solution.py:74
  122.5 39.2 %all-to-all-start.1 = ((f32[3,2,256,128]{3,1,0,2:T(2,128)}), f32[3,2,256,128]{3,1,0,2:T(2,128)S(1)}, u32[]{:S(2)}, u32[]{:S(2)}) async-start(f32[3,2,256,128]{3,1,0,2:T(2,128)} %copy.13), calls=%async_computation.1 | async-start | bytes 1572864 | tf_op jit(solution)/shard_map/all_to_all | solution.py:74
  126.4 19.8 %collective-permute-start.25 = (f32[2,32,2,128]{3,2,1,0:T(2,128)S(1)}, f32[2,32,2,128]{3,2,1,0:T(2,128)S(1)}, u32[]{:S(2)}, u32[]{:S(2)}) collective-permute-start(f32[2,32,2,128]{3,2,1,0:T(2,128)S(1)} %get-tuple-element.49), channel_id=1, source_target_pairs={{0,1},{1,2},{2,3},{3,4},{4,5},{5,6},{6,7},{7,8},{8,9},{9,10},{10,1... | collective-permute-start | bytes 196616 | tf_op jit(solution)/shard_map/ppermute | solution.py:40
  127.8 18.4 %collective-permute-start.26 = (f32[2,32,2,128]{3,2,1,0:T(2,128)S(1)}, f32[2,32,2,128]{3,2,1,0:T(2,128)S(1)}, u32[]{:S(2)}, u32[]{:S(2)}) collective-permute-start(f32[2,32,2,128]{3,2,1,0:T(2,128)S(1)} %get-tuple-element.50), channel_id=1, source_target_pairs={{1,0},{2,1},{3,2},{4,3},{5,4},{6,5},{7,6},{8,7},{9,8},{10,9},{11,1... | collective-permute-start | bytes 196616 | tf_op jit(solution)/shard_map/ppermute | solution.py:43
  130.1 9.4 %collective-permute-start.24 = (f32[2,2,16,128]{3,2,1,0:T(8,128)S(1)}, f32[2,2,16,128]{3,2,1,0:T(8,128)S(1)}, u32[]{:S(2)}, u32[]{:S(2)}) collective-permute-start(f32[2,2,16,128]{3,2,1,0:T(8,128)S(1)} %get-tuple-element.47), channel_id=1, source_target_pairs={{0,16},{16,32},{32,48},{48,64},{64,80},{80,96},{96,112},{112,128},... | collective-permute-start | bytes 98312 | tf_op jit(solution)/shard_map/ppermute | solution.py:46
  137.5 7.9 %collective-permute-start.27 = (f32[2,2,16,128]{3,2,1,0:T(8,128)S(1)}, f32[2,2,16,128]{3,2,1,0:T(8,128)S(1)}, u32[]{:S(2)}, u32[]{:S(2)}) collective-permute-start(f32[2,2,16,128]{3,2,1,0:T(8,128)S(1)} %get-tuple-element.48), channel_id=1, source_target_pairs={{16,0},{32,16},{48,32},{64,48},{80,64},{96,80},{112,96},{128,112},... | collective-permute-start | bytes 98312 | tf_op jit(solution)/shard_map/ppermute | solution.py:49
  147.7 21.7 %collective-permute-start.29 = (f32[2,32,2,128]{3,2,1,0:T(2,128)S(1)}, f32[2,32,2,128]{3,2,1,0:T(2,128)S(1)}, u32[]{:S(2)}, u32[]{:S(2)}) collective-permute-start(f32[2,32,2,128]{3,2,1,0:T(2,128)S(1)} %get-tuple-element.45), channel_id=1, source_target_pairs={{0,1},{1,2},{2,3},{3,4},{4,5},{5,6},{6,7},{7,8},{8,9},{9,10},{10,1... | collective-permute-start | bytes 196616 | tf_op jit(solution)/shard_map/ppermute | solution.py:40
  149.0 26.6 %collective-permute-start.30 = (f32[2,32,2,128]{3,2,1,0:T(2,128)S(1)}, f32[2,32,2,128]{3,2,1,0:T(2,128)S(1)}, u32[]{:S(2)}, u32[]{:S(2)}) collective-permute-start(f32[2,32,2,128]{3,2,1,0:T(2,128)S(1)} %get-tuple-element.46), channel_id=1, source_target_pairs={{1,0},{2,1},{3,2},{4,3},{5,4},{6,5},{7,6},{8,7},{9,8},{10,9},{11,1... | collective-permute-start | bytes 196616 | tf_op jit(solution)/shard_map/ppermute | solution.py:43
  151.4 11.1 %collective-permute-start.28 = (f32[2,2,16,128]{3,2,1,0:T(8,128)S(1)}, f32[2,2,16,128]{3,2,1,0:T(8,128)S(1)}, u32[]{:S(2)}, u32[]{:S(2)}) collective-permute-start(f32[2,2,16,128]{3,2,1,0:T(8,128)S(1)} %get-tuple-element.43), channel_id=1, source_target_pairs={{0,16},{16,32},{32,48},{48,64},{64,80},{80,96},{96,112},{112,128},... | collective-permute-start | bytes 98312 | tf_op jit(solution)/shard_map/ppermute | solution.py:46
  159.8 7.6 %collective-permute-start.31 = (f32[2,2,16,128]{3,2,1,0:T(8,128)S(1)}, f32[2,2,16,128]{3,2,1,0:T(8,128)S(1)}, u32[]{:S(2)}, u32[]{:S(2)}) collective-permute-start(f32[2,2,16,128]{3,2,1,0:T(8,128)S(1)} %get-tuple-element.44), channel_id=1, source_target_pairs={{16,0},{32,16},{48,32},{64,48},{80,64},{96,80},{112,96},{128,112},... | collective-permute-start | bytes 98312 | tf_op jit(solution)/shard_map/ppermute | solution.py:49
  162.0 14.6 %collective-permute-start.10 = (f32[3,32,2,128]{3,2,1,0:T(2,128)S(1)}, f32[3,32,2,128]{3,2,1,0:T(2,128)S(1)}, u32[]{:S(2)}, u32[]{:S(2)}) collective-permute-start(f32[3,32,2,128]{3,2,1,0:T(2,128)S(1)} %get-tuple-element.28), channel_id=1, source_target_pairs={{1,0},{2,1},{3,2},{4,3},{5,4},{6,5},{7,6},{8,7},{9,8},{10,9},{11,1... | collective-permute-start | bytes 294920 | tf_op jit(solution)/shard_map/ppermute | solution.py:43
  162.4 14.2 %collective-permute-start.9 = (f32[3,32,2,128]{3,2,1,0:T(2,128)S(1)}, f32[3,32,2,128]{3,2,1,0:T(2,128)S(1)}, u32[]{:S(2)}, u32[]{:S(2)}) collective-permute-start(f32[3,32,2,128]{3,2,1,0:T(2,128)S(1)} %get-tuple-element.27), channel_id=1, source_target_pairs={{0,1},{1,2},{2,3},{3,4},{4,5},{5,6},{6,7},{7,8},{8,9},{9,10},{10,1... | collective-permute-start | bytes 294920 | tf_op jit(solution)/shard_map/ppermute | solution.py:40
  167.4 8.4 %collective-permute-start.11 = (f32[3,2,16,128]{3,2,1,0:T(8,128)S(1)}, f32[3,2,16,128]{3,2,1,0:T(8,128)S(1)}, u32[]{:S(2)}, u32[]{:S(2)}) collective-permute-start(f32[3,2,16,128]{3,2,1,0:T(8,128)S(1)} %get-tuple-element.26), channel_id=1, source_target_pairs={{16,0},{32,16},{48,32},{64,48},{80,64},{96,80},{112,96},{128,112},... | collective-permute-start | bytes 147464 | tf_op jit(solution)/shard_map/ppermute | solution.py:49
  169.4 7.2 %collective-permute-start.8 = (f32[3,2,16,128]{3,2,1,0:T(8,128)S(1)}, f32[3,2,16,128]{3,2,1,0:T(8,128)S(1)}, u32[]{:S(2)}, u32[]{:S(2)}) collective-permute-start(f32[3,2,16,128]{3,2,1,0:T(8,128)S(1)} %get-tuple-element.25), channel_id=1, source_target_pairs={{0,16},{16,32},{32,48},{48,64},{64,80},{80,96},{96,112},{112,128},... | collective-permute-start | bytes 147464 | tf_op jit(solution)/shard_map/ppermute | solution.py:46
  179.0 18.7 %collective-permute-start.13 = (f32[3,32,2,128]{3,2,1,0:T(2,128)S(1)}, f32[3,32,2,128]{3,2,1,0:T(2,128)S(1)}, u32[]{:S(2)}, u32[]{:S(2)}) collective-permute-start(f32[3,32,2,128]{3,2,1,0:T(2,128)S(1)} %get-tuple-element.23), channel_id=1, source_target_pairs={{0,1},{1,2},{2,3},{3,4},{4,5},{5,6},{6,7},{7,8},{8,9},{9,10},{10,1... | collective-permute-start | bytes 294920 | tf_op jit(solution)/shard_map/ppermute | solution.py:40
  179.1 18.6 %collective-permute-start.14 = (f32[3,32,2,128]{3,2,1,0:T(2,128)S(1)}, f32[3,32,2,128]{3,2,1,0:T(2,128)S(1)}, u32[]{:S(2)}, u32[]{:S(2)}) collective-permute-start(f32[3,32,2,128]{3,2,1,0:T(2,128)S(1)} %get-tuple-element.24), channel_id=1, source_target_pairs={{1,0},{2,1},{3,2},{4,3},{5,4},{6,5},{7,6},{8,7},{9,8},{10,9},{11,1... | collective-permute-start | bytes 294920 | tf_op jit(solution)/shard_map/ppermute | solution.py:43
  182.7 10.4 %collective-permute-start.12 = (f32[3,2,16,128]{3,2,1,0:T(8,128)S(1)}, f32[3,2,16,128]{3,2,1,0:T(8,128)S(1)}, u32[]{:S(2)}, u32[]{:S(2)}) collective-permute-start(f32[3,2,16,128]{3,2,1,0:T(8,128)S(1)} %get-tuple-element.21), channel_id=1, source_target_pairs={{0,16},{16,32},{32,48},{48,64},{64,80},{80,96},{96,112},{112,128},... | collective-permute-start | bytes 147464 | tf_op jit(solution)/shard_map/ppermute | solution.py:46
  189.9 7.8 %collective-permute-start.15 = (f32[3,2,16,128]{3,2,1,0:T(8,128)S(1)}, f32[3,2,16,128]{3,2,1,0:T(8,128)S(1)}, u32[]{:S(2)}, u32[]{:S(2)}) collective-permute-start(f32[3,2,16,128]{3,2,1,0:T(8,128)S(1)} %get-tuple-element.22), channel_id=1, source_target_pairs={{16,0},{32,16},{48,32},{64,48},{80,64},{96,80},{112,96},{128,112},... | collective-permute-start | bytes 147464 | tf_op jit(solution)/shard_map/ppermute | solution.py:49
where the time goes:
time: 202 us; the launch traced here: 201 us
  starting transfers between devices  116 us (57%)
  waiting for transfers between devices  53.3 us (26%)
  other arithmetic  17.7 us (9%)
  local copies, waits for them, and re-layouts  10.2 us (5%)
  between operations  4.4 us (2%)
    ppermute x8, starting transfers between devices, extend(): lax.ppermute(cells[..., rows - width:, :, :], 'rad', [(i, i + 1) for i in...  50.5 us
    ppermute x8, waiting for transfers between devices, extend(): lax.ppermute(cells[..., :width, :, :], 'rad', [(i + 1, i) for i in range(...  22.5 us
    ppermute x8, starting transfers between devices, extend(): lax.ppermute(cells[..., :width, :], 'azi', [((i + 1) % sectors, i) for i...  21.3 us
    ppermute x8, starting transfers between devices, extend(): lax.ppermute(cells[..., :width, :, :], 'rad', [(i + 1, i) for i in range(...  15.5 us
    all_to_all x2, waiting for transfers between devices, shift_rows(): return lax.all_to_all(moved, 'azi', 2, 1, tiled=True)  14.7 us
    all_to_all x2, waiting for transfers between devices, shift_rows(): full = lax.all_to_all(half, 'azi', 1, 2, tiled=True)  14.5 us
    all_to_all x2, starting transfers between devices, shift_rows(): full = lax.all_to_all(half, 'azi', 1, 2, tiled=True)  13.6 us
    ppermute x8, starting transfers between devices, extend(): lax.ppermute(cells[..., cols - width:, :], 'azi', [(i, (i + 1) % sectors)...  7.44 us
  transfers between devices with their start and end apart: 36, of which 10 were waited for; matrix products, arithmetic and copies ran while one was open for 10% of the time, Pallas kernels for 0%

commit v1 on v0

--- a/solution.py
+++ b/solution.py
@@ -61,7 +61,10 @@
     peers = lax.axis_size("azi")
     rows = half.shape[1]
     per = rows // peers
-    full = lax.all_to_all(half, "azi", 1, 2, tiled=True)
+    full = jnp.concatenate(
+        lax.all_to_all(jnp.stack(jnp.split(half, lax.axis_size("azi"), axis=1)), "azi", 0, 0),
+        axis=2,
+    )
     length = full.shape[2]
     first = lax.axis_index("azi") * per
     mine = lax.dynamic_slice_in_dim(shifts, first, per)

time: 202 us -> 212 us (1.050)
  the two profiles are of different devices: /device:TPU:17 before, /device:TPU:1 now
where the time goes in v1:
time: 212 us; the launch traced here: 211 us
  starting transfers between devices  115 us (54%)
  waiting for transfers between devices  46.2 us (22%)
  local copies, waits for them, and re-layouts  28.2 us (13%)
  other arithmetic  17.7 us (8%)
  between operations  4.47 us (2%)
    ppermute x8, starting transfers between devices, extend(): lax.ppermute(cells[..., rows - width:, :, :], 'rad', [(i, i + 1) for i in...  52.1 us
    ppermute x8, starting transfers between devices, extend(): lax.ppermute(cells[..., :width, :], 'azi', [((i + 1) % sectors, i) for i...  20.9 us
    unnamed x38, local copies, waits for them, and re-layouts  18.5 us
    all_to_all x2, waiting for transfers between devices, shift_rows(): lax.all_to_all(jnp.stack(jnp.split(half, lax.axis_size('azi'), axis=1)),...  16.1 us
    ppermute x8, starting transfers between devices, extend(): lax.ppermute(cells[..., :width, :, :], 'rad', [(i + 1, i) for i in range(...  15.4 us
    all_to_all x2, waiting for transfers between devices, shift_rows(): return lax.all_to_all(moved, 'azi', 2, 1, tiled=True)  14.8 us
    ppermute x8, waiting for transfers between devices, extend(): lax.ppermute(cells[..., :width, :, :], 'rad', [(i + 1, i) for i in range(...  14.5 us
    all_to_all x2, starting transfers between devices, shift_rows(): lax.all_to_all(jnp.stack(jnp.split(half, lax.axis_size('azi'), axis=1)),...  11.3 us
  transfers between devices with their start and end apart: 36, of which 9 were waited for; matrix products, arithmetic and copies ran while one was open for 18% of the time, Pallas kernels for 0%

profile of v1, /device:TPU:1, one launch (start us, length us, event | category | flops | bytes accessed | tf_op | source)
XLA Modules:
  0.0 211.3 jit_solution(5706859375521280054)
XLA Ops:
  0.0 1.3 fusion.119
  1.3 2.2 %collective-permute-start.1 = (f32[3,32,2,128]{3,2,1,0:T(2,128)S(1)}, f32[3,32,2,128]{3,2,1,0:T(2,128)S(1)}, u32[]{:S(2)}, u32[]{:S(2)}) collective-permute-start(f32[3,32,2,128]{3,2,1,0:T(2,128)S(1)} %get-tuple-element.7), channel_id=1, source_target_pairs={{0,1},{1,2},{2,3},{3,4},{4,5},{5,6},{6,7},{7,8},{8,9},{9,10},{10,1... | collective-permute-start | bytes 294920 | tf_op jit(solution)/shard_map/ppermute | solution.py:40
  3.5 1.1 fusion.121
  4.6 1.6 collective-permute-start.17
  6.2 3.9 %collective-permute-start.18 = (f32[2,32,2,128]{3,2,1,0:T(2,128)S(1)}, f32[2,32,2,128]{3,2,1,0:T(2,128)S(1)}, u32[]{:S(2)}, u32[]{:S(2)}) collective-permute-start(f32[2,32,2,128]{3,2,1,0:T(2,128)S(1)} %get-tuple-element.12), channel_id=1, source_target_pairs={{1,0},{2,1},{3,2},{4,3},{5,4},{6,5},{7,6},{8,7},{9,8},{10,9},{11,1... | collective-permute-start | bytes 196616 | tf_op jit(solution)/shard_map/ppermute | solution.py:43
  10.1 0.8 fusion.120
  10.8 5.4 %collective-permute-start.16 = (f32[2,2,16,128]{3,2,1,0:T(8,128)S(1)}, f32[2,2,16,128]{3,2,1,0:T(8,128)S(1)}, u32[]{:S(2)}, u32[]{:S(2)}) collective-permute-start(f32[2,2,16,128]{3,2,1,0:T(8,128)S(1)} %get-tuple-element.9), channel_id=1, source_target_pairs={{0,16},{16,32},{32,48},{48,64},{64,80},{80,96},{96,112},{112,128},... | collective-permute-start | bytes 98312 | tf_op jit(solution)/shard_map/ppermute | solution.py:46
  16.2 1.9 collective-permute-start.19
  18.1 0.8 fusion.118
  19.0 1.0 broadcast_multiply_fusion
  20.1 1.2 collective-permute-start.2
  21.3 2.2 %collective-permute-done.19 = f32[2,2,16,128]{3,2,1,0:T(8,128)S(1)} collective-permute-done((f32[2,2,16,128]{3,2,1,0:T(8,128)S(1)}, f32[2,2,16,128]{3,2,1,0:T(8,128)S(1)}, u32[]{:S(2)}, u32[]{:S(2)}) %collective-permute-start.19) | collective-permute-done | bytes 32800 | tf_op jit(solution)/shard_map/ppermute | solution.py:49
  23.5 3.9 %collective-permute-start = (f32[3,2,16,128]{3,2,1,0:T(8,128)S(1)}, f32[3,2,16,128]{3,2,1,0:T(8,128)S(1)}, u32[]{:S(2)}, u32[]{:S(2)}) collective-permute-start(f32[3,2,16,128]{3,2,1,0:T(8,128)S(1)} %get-tuple-element.5), channel_id=1, source_target_pairs={{0,16},{16,32},{32,48},{48,64},{64,80},{80,96},{96,112},{112,128},... | collective-permute-start | bytes 147464 | tf_op jit(solution)/shard_map/ppermute | solution.py:46
  27.4 1.9 collective-permute-start.3
  29.5 1.2 fusion.74
  30.9 3.6 %collective-permute-start.22 = (f32[2,32,2,128]{3,2,1,0:T(2,128)S(1)}, f32[2,32,2,128]{3,2,1,0:T(2,128)S(1)}, u32[]{:S(2)}, u32[]{:S(2)}) collective-permute-start(f32[2,32,2,128]{3,2,1,0:T(2,128)S(1)} %get-tuple-element.56), channel_id=1, source_target_pairs={{1,0},{2,1},{3,2},{4,3},{5,4},{6,5},{7,6},{8,7},{9,8},{10,9},{11,1... | collective-permute-start | bytes 196616 | tf_op jit(solution)/shard_map/ppermute | solution.py:43
  34.6 5.6 %collective-permute-start.20 = (f32[2,2,16,128]{3,2,1,0:T(8,128)S(1)}, f32[2,2,16,128]{3,2,1,0:T(8,128)S(1)}, u32[]{:S(2)}, u32[]{:S(2)}) collective-permute-start(f32[2,2,16,128]{3,2,1,0:T(8,128)S(1)} %get-tuple-element.53), channel_id=1, source_target_pairs={{0,16},{16,32},{32,48},{48,64},{64,80},{80,96},{96,112},{112,128},... | collective-permute-start | bytes 98312 | tf_op jit(solution)/shard_map/ppermute | solution.py:46
  40.1 1.9 collective-permute-start.23
  42.3 2.1 fusion.16
  44.6 3.6 %collective-permute-start.6 = (f32[3,32,2,128]{3,2,1,0:T(2,128)S(1)}, f32[3,32,2,128]{3,2,1,0:T(2,128)S(1)}, u32[]{:S(2)}, u32[]{:S(2)}) collective-permute-start(f32[3,32,2,128]{3,2,1,0:T(2,128)S(1)} %get-tuple-element.34), channel_id=1, source_target_pairs={{1,0},{2,1},{3,2},{4,3},{5,4},{6,5},{7,6},{8,7},{9,8},{10,9},{11,1... | collective-permute-start | bytes 294920 | tf_op jit(solution)/shard_map/ppermute | solution.py:43
  48.2 5.7 %collective-permute-start.4 = (f32[3,2,16,128]{3,2,1,0:T(8,128)S(1)}, f32[3,2,16,128]{3,2,1,0:T(8,128)S(1)}, u32[]{:S(2)}, u32[]{:S(2)}) collective-permute-start(f32[3,2,16,128]{3,2,1,0:T(8,128)S(1)} %get-tuple-element.31), channel_id=1, source_target_pairs={{0,16},{16,32},{32,48},{48,64},{64,80},{80,96},{96,112},{112,128},... | collective-permute-start | bytes 147464 | tf_op jit(solution)/shard_map/ppermute | solution.py:46
  53.9 1.9 collective-permute-start.7
  56.0 1.3 fusion.86
  67.1 5.8 %all-to-all-start.2 = ((f32[16,2,2,16,128]{4,3,2,1,0:T(8,128)}), f32[16,2,2,16,128]{4,3,2,1,0:T(8,128)S(1)}, u32[]{:S(2)}, u32[]{:S(2)}) async-start(f32[16,2,2,16,128]{4,3,2,1,0:T(8,128)} %constant_dynamic-update-slice_fusion.16), calls=%async_computation.2 | async-start | bytes 1048576 | tf_op jit(solution)/shard_map/all_to_all | solution.py:65
  73.1 2.1 %fusion.28 = f32[3,32,16,128]{3,2,1,0:T(8,128)S(1)} fusion(f32[3,32,16,128]{3,2,1,0:T(8,128)S(1)} %fusion.16, f32[3,32,2,128]{3,2,1,0:T(2,128)S(1)} %collective-permute-done.6, f32[3,32,2,128]{3,2,1,0:T(2,128)S(1)} %collective-permute-done.5, f32[3,34,20,128]{3,2,1,0:T(8,128)S(1)} %get-tuple-element.18, f32[3,34,20,128]{3,2,1,0:T(8,128)S(1)} %get-tuple-element.17, ...), kind=kLoop, calls=%fused_computation.101 | loop fusion | flops 9043968 | bytes 5964544 | tf_op jit(solution)/shard_map/mul | solution.py:57
  75.3 0.6 constant_dynamic-update-slice_fusion.15
  75.9 0.6 constant_dynamic-update-slice_fusion.14
  76.5 0.6 constant_dynamic-update-slice_fusion.13
  77.2 0.6 constant_dynamic-update-slice_fusion.12
  77.8 0.6 constant_dynamic-update-slice_fusion.11
  78.4 0.6 constant_dynamic-update-slice_fusion.10
  79.0 0.6 constant_dynamic-update-slice_fusion.9
  79.6 0.6 constant_dynamic-update-slice_fusion.8
  85.3 2.0 all-to-all-done.2
  87.2 5.6 %all-to-all-start = ((f32[16,3,2,16,128]{4,3,2,1,0:T(8,128)}), f32[16,3,2,16,128]{4,3,2,1,0:T(8,128)S(1)}, u32[]{:S(2)}, u32[]{:S(2)}) async-start(f32[16,3,2,16,128]{4,3,2,1,0:T(8,128)} %constant_dynamic-update-slice_fusion), calls=%async_computation | async-start | bytes 1572864 | tf_op jit(solution)/shard_map/all_to_all | solution.py:65
  97.6 1.2 copy.50
  98.8 14.1 %all-to-all-done = f32[16,3,2,16,128]{4,3,2,1,0:T(8,128)S(1)} async-done(((f32[16,3,2,16,128]{4,3,2,1,0:T(8,128)}), f32[16,3,2,16,128]{4,3,2,1,0:T(8,128)S(1)}, u32[]{:S(2)}, u32[]{:S(2)}) %all-to-all-start) | async-done | bytes 786464 | tf_op jit(solution)/shard_map/all_to_all | solution.py:65
  112.9 3.6 %all-to-all-start.3 = ((f32[2,2,256,128]{3,1,0,2:T(2,128)}), f32[2,2,256,128]{3,1,0,2:T(2,128)S(1)}, u32[]{:S(2)}, u32[]{:S(2)}) async-start(f32[2,2,256,128]{3,1,0,2:T(2,128)} %copy.50), calls=%async_computation.3 | async-start | bytes 1048576 | tf_op jit(solution)/shard_map/all_to_all | solution.py:77
  117.0 1.5 copy.46
  118.5 14.8 %all-to-all-done.3 = f32[2,2,256,128]{3,1,0,2:T(2,128)S(1)} async-done(((f32[2,2,256,128]{3,1,0,2:T(2,128)}), f32[2,2,256,128]{3,1,0,2:T(2,128)S(1)}, u32[]{:S(2)}, u32[]{:S(2)}) %all-to-all-start.3) | async-done | bytes 524320 | tf_op jit(solution)/shard_map/all_to_all | solution.py:77
  133.2 3.6 %all-to-all-start.1 = ((f32[3,2,256,128]{3,1,0,2:T(2,128)}), f32[3,2,256,128]{3,1,0,2:T(2,128)S(1)}, u32[]{:S(2)}, u32[]{:S(2)}) async-start(f32[3,2,256,128]{3,1,0,2:T(2,128)} %copy.46), calls=%async_computation.1 | async-start | bytes 1572864 | tf_op jit(solution)/shard_map/all_to_all | solution.py:77
  137.1 1.4 collective-permute-start.25
  138.5 2.2 %collective-permute-start.26 = (f32[2,32,2,128]{3,2,1,0:T(2,128)S(1)}, f32[2,32,2,128]{3,2,1,0:T(2,128)S(1)}, u32[]{:S(2)}, u32[]{:S(2)}) collective-permute-start(f32[2,32,2,128]{3,2,1,0:T(2,128)S(1)} %get-tuple-element.50), channel_id=1, source_target_pairs={{1,0},{2,1},{3,2},{4,3},{5,4},{6,5},{7,6},{8,7},{9,8},{10,9},{11,1... | collective-permute-start | bytes 196616 | tf_op jit(solution)/shard_map/ppermute | solution.py:43
  140.7 9.8 %collective-permute-start.24 = (f32[2,2,16,128]{3,2,1,0:T(8,128)S(1)}, f32[2,2,16,128]{3,2,1,0:T(8,128)S(1)}, u32[]{:S(2)}, u32[]{:S(2)}) collective-permute-start(f32[2,2,16,128]{3,2,1,0:T(8,128)S(1)} %get-tuple-element.47), channel_id=1, source_target_pairs={{0,16},{16,32},{32,48},{48,64},{64,80},{80,96},{96,112},{112,128},... | collective-permute-start | bytes 98312 | tf_op jit(solution)/shard_map/ppermute | solution.py:46
  150.5 1.9 collective-permute-start.27
  152.5 4.9 %collective-permute-done.27 = f32[2,2,16,128]{3,2,1,0:T(8,128)S(1)} collective-permute-done((f32[2,2,16,128]{3,2,1,0:T(8,128)S(1)}, f32[2,2,16,128]{3,2,1,0:T(8,128)S(1)}, u32[]{:S(2)}, u32[]{:S(2)}) %collective-permute-start.27) | collective-permute-done | bytes 32800 | tf_op jit(solution)/shard_map/ppermute | solution.py:49
  157.6 1.2 fusion.97
  158.9 0.8 collective-permute-start.29
  159.6 2.9 %collective-permute-start.30 = (f32[2,32,2,128]{3,2,1,0:T(2,128)S(1)}, f32[2,32,2,128]{3,2,1,0:T(2,128)S(1)}, u32[]{:S(2)}, u32[]{:S(2)}) collective-permute-start(f32[2,32,2,128]{3,2,1,0:T(2,128)S(1)} %get-tuple-element.46), channel_id=1, source_target_pairs={{1,0},{2,1},{3,2},{4,3},{5,4},{6,5},{7,6},{8,7},{9,8},{10,9},{11,1... | collective-permute-start | bytes 196616 | tf_op jit(solution)/shard_map/ppermute | solution.py:43
  162.5 10.2 %collective-permute-start.28 = (f32[2,2,16,128]{3,2,1,0:T(8,128)S(1)}, f32[2,2,16,128]{3,2,1,0:T(8,128)S(1)}, u32[]{:S(2)}, u32[]{:S(2)}) collective-permute-start(f32[2,2,16,128]{3,2,1,0:T(8,128)S(1)} %get-tuple-element.43), channel_id=1, source_target_pairs={{0,16},{16,32},{32,48},{48,64},{64,80},{80,96},{96,112},{112,128},... | collective-permute-start | bytes 98312 | tf_op jit(solution)/shard_map/ppermute | solution.py:46
  172.7 1.9 collective-permute-start.31
  175.0 1.4 collective-permute-start.9
  176.5 3.6 %collective-permute-done.31 = f32[2,2,16,128]{3,2,1,0:T(8,128)S(1)} collective-permute-done((f32[2,2,16,128]{3,2,1,0:T(8,128)S(1)}, f32[2,2,16,128]{3,2,1,0:T(8,128)S(1)}, u32[]{:S(2)}, u32[]{:S(2)}) %collective-permute-start.31) | collective-permute-done | bytes 32800 | tf_op jit(solution)/shard_map/ppermute | solution.py:49
  180.1 1.9 collective-permute-start.11
  182.0 5.4 %collective-permute-start.8 = (f32[3,2,16,128]{3,2,1,0:T(8,128)S(1)}, f32[3,2,16,128]{3,2,1,0:T(8,128)S(1)}, u32[]{:S(2)}, u32[]{:S(2)}) collective-permute-start(f32[3,2,16,128]{3,2,1,0:T(8,128)S(1)} %get-tuple-element.25), channel_id=1, source_target_pairs={{0,16},{16,32},{32,48},{48,64},{64,80},{80,96},{96,112},{112,128},... | collective-permute-start | bytes 147464 | tf_op jit(solution)/shard_map/ppermute | solution.py:46
  187.6 0.8 collective-permute-done.8
  188.6 2.1 fusion.39
  190.9 3.6 %collective-permute-start.14 = (f32[3,32,2,128]{3,2,1,0:T(2,128)S(1)}, f32[3,32,2,128]{3,2,1,0:T(2,128)S(1)}, u32[]{:S(2)}, u32[]{:S(2)}) collective-permute-start(f32[3,32,2,128]{3,2,1,0:T(2,128)S(1)} %get-tuple-element.24), channel_id=1, source_target_pairs={{1,0},{2,1},{3,2},{4,3},{5,4},{6,5},{7,6},{8,7},{9,8},{10,9},{11,1... | collective-permute-start | bytes 294920 | tf_op jit(solution)/shard_map/ppermute | solution.py:43
  194.4 6.3 %collective-permute-start.12 = (f32[3,2,16,128]{3,2,1,0:T(8,128)S(1)}, f32[3,2,16,128]{3,2,1,0:T(8,128)S(1)}, u32[]{:S(2)}, u32[]{:S(2)}) collective-permute-start(f32[3,2,16,128]{3,2,1,0:T(8,128)S(1)} %get-tuple-element.21), channel_id=1, source_target_pairs={{0,16},{16,32},{32,48},{48,64},{64,80},{80,96},{96,112},{112,128},... | collective-permute-start | bytes 147464 | tf_op jit(solution)/shard_map/ppermute | solution.py:46
  200.7 1.9 collective-permute-start.15
  202.7 1.3 fusion.109
  204.0 3.7 %collective-permute-done.15 = f32[3,2,16,128]{3,2,1,0:T(8,128)S(1)} collective-permute-done((f32[3,2,16,128]{3,2,1,0:T(8,128)S(1)}, f32[3,2,16,128]{3,2,1,0:T(8,128)S(1)}, u32[]{:S(2)}, u32[]{:S(2)}) %collective-permute-start.15) | collective-permute-done | bytes 49184 | tf_op jit(solution)/shard_map/ppermute | solution.py:49
  207.9 2.2 %fusion.51 = f32[3,32,16,128]{3,2,1,0:T(8,128)S(1)} fusion(f32[3,32,16,128]{3,2,1,0:T(8,128)S(1)} %fusion.39, f32[3,32,2,128]{3,2,1,0:T(2,128)S(1)} %collective-permute-done.14, f32[3,32,2,128]{3,2,1,0:T(2,128)S(1)} %collective-permute-done.13, f32[3,34,20,128]{3,2,1,0:T(8,128)S(1)} %get-tuple-element.14, f32[3,34,20,128]{3,2,1,0:T(8,128)S(1)} %get-tuple-element.13, ...), kind=kLoop, calls=%fused_computation.124 | loop fusion | flops 9043968 | bytes 5964544 | tf_op jit(solution)/shard_map/mul | solution.py:57
  210.1 1.2 pad_maximum_fusion
  (104 shorter events, 19.0 us)
Async XLA Ops:
  0.0 20.0 %copy-start = (f32[5,32,16,128]{3,2,1,0:T(8,128)S(1)}, f32[5,32,16,128]{3,2,1,0:T(8,128)}, u32[]{:S(2)}) copy-start(f32[5,32,16,128]{3,2,1,0:T(8,128)} %param.5) | copy-start | bytes 3932164
  0.0 19.9 %copy-start.2 = (f32[5,32]{1,0:T(8,128)S(1)}, f32[5,32]{1,0:T(8,128)}, u32[]{:S(2)}) copy-start(f32[5,32]{1,0:T(8,128)} %param.7) | copy-start | bytes 1924
  0.0 20.0 %copy-start.1 = (f32[5,32]{1,0:T(8,128)S(1)}, f32[5,32]{1,0:T(8,128)}, u32[]{:S(2)}) copy-start(f32[5,32]{1,0:T(8,128)} %param.8) | copy-start | bytes 1924
  1.3 38.8 %collective-permute-start.1 = (f32[3,32,2,128]{3,2,1,0:T(2,128)S(1)}, f32[3,32,2,128]{3,2,1,0:T(2,128)S(1)}, u32[]{:S(2)}, u32[]{:S(2)}) collective-permute-start(f32[3,32,2,128]{3,2,1,0:T(2,128)S(1)} %get-tuple-element.7), channel_id=1, source_target_pairs={{0,1},{1,2},{2,3},{3,4},{4,5},{5,6},{6,7},{7,8},{8,9},{9,10},{10,1... | collective-permute-start | bytes 294920 | tf_op jit(solution)/shard_map/ppermute | solution.py:40
  4.6 22.8 %collective-permute-start.17 = (f32[2,32,2,128]{3,2,1,0:T(2,128)S(1)}, f32[2,32,2,128]{3,2,1,0:T(2,128)S(1)}, u32[]{:S(2)}, u32[]{:S(2)}) collective-permute-start(f32[2,32,2,128]{3,2,1,0:T(2,128)S(1)} %get-tuple-element.11), channel_id=1, source_target_pairs={{0,1},{1,2},{2,3},{3,4},{4,5},{5,6},{6,7},{7,8},{8,9},{9,10},{10,1... | collective-permute-start | bytes 196616 | tf_op jit(solution)/shard_map/ppermute | solution.py:40
  6.2 23.1 %collective-permute-start.18 = (f32[2,32,2,128]{3,2,1,0:T(2,128)S(1)}, f32[2,32,2,128]{3,2,1,0:T(2,128)S(1)}, u32[]{:S(2)}, u32[]{:S(2)}) collective-permute-start(f32[2,32,2,128]{3,2,1,0:T(2,128)S(1)} %get-tuple-element.12), channel_id=1, source_target_pairs={{1,0},{2,1},{3,2},{4,3},{5,4},{6,5},{7,6},{8,7},{9,8},{10,9},{11,1... | collective-permute-start | bytes 196616 | tf_op jit(solution)/shard_map/ppermute | solution.py:43
  10.8 9.3 %collective-permute-start.16 = (f32[2,2,16,128]{3,2,1,0:T(8,128)S(1)}, f32[2,2,16,128]{3,2,1,0:T(8,128)S(1)}, u32[]{:S(2)}, u32[]{:S(2)}) collective-permute-start(f32[2,2,16,128]{3,2,1,0:T(8,128)S(1)} %get-tuple-element.9), channel_id=1, source_target_pairs={{0,16},{16,32},{32,48},{48,64},{64,80},{80,96},{96,112},{112,128},... | collective-permute-start | bytes 98312 | tf_op jit(solution)/shard_map/ppermute | solution.py:46
  16.2 7.3 %collective-permute-start.19 = (f32[2,2,16,128]{3,2,1,0:T(8,128)S(1)}, f32[2,2,16,128]{3,2,1,0:T(8,128)S(1)}, u32[]{:S(2)}, u32[]{:S(2)}) collective-permute-start(f32[2,2,16,128]{3,2,1,0:T(8,128)S(1)} %get-tuple-element.10), channel_id=1, source_target_pairs={{16,0},{32,16},{48,32},{64,48},{80,64},{96,80},{112,96},{128,112},... | collective-permute-start | bytes 98312 | tf_op jit(solution)/shard_map/ppermute | solution.py:49
  20.1 22.0 %collective-permute-start.2 = (f32[3,32,2,128]{3,2,1,0:T(2,128)S(1)}, f32[3,32,2,128]{3,2,1,0:T(2,128)S(1)}, u32[]{:S(2)}, u32[]{:S(2)}) collective-permute-start(f32[3,32,2,128]{3,2,1,0:T(2,128)S(1)} %get-tuple-element.8), channel_id=1, source_target_pairs={{1,0},{2,1},{3,2},{4,3},{5,4},{6,5},{7,6},{8,7},{9,8},{10,9},{11,1... | collective-permute-start | bytes 294920 | tf_op jit(solution)/shard_map/ppermute | solution.py:43
  23.5 7.4 %collective-permute-start = (f32[3,2,16,128]{3,2,1,0:T(8,128)S(1)}, f32[3,2,16,128]{3,2,1,0:T(8,128)S(1)}, u32[]{:S(2)}, u32[]{:S(2)}) collective-permute-start(f32[3,2,16,128]{3,2,1,0:T(8,128)S(1)} %get-tuple-element.5), channel_id=1, source_target_pairs={{0,16},{16,32},{32,48},{48,64},{64,80},{80,96},{96,112},{112,128},... | collective-permute-start | bytes 147464 | tf_op jit(solution)/shard_map/ppermute | solution.py:46
  27.4 7.2 %collective-permute-start.3 = (f32[3,2,16,128]{3,2,1,0:T(8,128)S(1)}, f32[3,2,16,128]{3,2,1,0:T(8,128)S(1)}, u32[]{:S(2)}, u32[]{:S(2)}) collective-permute-start(f32[3,2,16,128]{3,2,1,0:T(8,128)S(1)} %get-tuple-element.6), channel_id=1, source_target_pairs={{16,0},{32,16},{48,32},{64,48},{80,64},{96,80},{112,96},{128,112},... | collective-permute-start | bytes 147464 | tf_op jit(solution)/shard_map/ppermute | solution.py:49
  30.8 23.1 %collective-permute-start.21 = (f32[2,32,2,128]{3,2,1,0:T(2,128)S(1)}, f32[2,32,2,128]{3,2,1,0:T(2,128)S(1)}, u32[]{:S(2)}, u32[]{:S(2)}) collective-permute-start(f32[2,32,2,128]{3,2,1,0:T(2,128)S(1)} %get-tuple-element.55), channel_id=1, source_target_pairs={{0,1},{1,2},{2,3},{3,4},{4,5},{5,6},{6,7},{7,8},{8,9},{9,10},{10,1... | collective-permute-start | bytes 196616 | tf_op jit(solution)/shard_map/ppermute | solution.py:40
  30.9 25.0 %collective-permute-start.22 = (f32[2,32,2,128]{3,2,1,0:T(2,128)S(1)}, f32[2,32,2,128]{3,2,1,0:T(2,128)S(1)}, u32[]{:S(2)}, u32[]{:S(2)}) collective-permute-start(f32[2,32,2,128]{3,2,1,0:T(2,128)S(1)} %get-tuple-element.56), channel_id=1, source_target_pairs={{1,0},{2,1},{3,2},{4,3},{5,4},{6,5},{7,6},{8,7},{9,8},{10,9},{11,1... | collective-permute-start | bytes 196616 | tf_op jit(solution)/shard_map/ppermute | solution.py:43
  34.6 10.0 %collective-permute-start.20 = (f32[2,2,16,128]{3,2,1,0:T(8,128)S(1)}, f32[2,2,16,128]{3,2,1,0:T(8,128)S(1)}, u32[]{:S(2)}, u32[]{:S(2)}) collective-permute-start(f32[2,2,16,128]{3,2,1,0:T(8,128)S(1)} %get-tuple-element.53), channel_id=1, source_target_pairs={{0,16},{16,32},{32,48},{48,64},{64,80},{80,96},{96,112},{112,128},... | collective-permute-start | bytes 98312 | tf_op jit(solution)/shard_map/ppermute | solution.py:46
  40.1 8.0 %collective-permute-start.23 = (f32[2,2,16,128]{3,2,1,0:T(8,128)S(1)}, f32[2,2,16,128]{3,2,1,0:T(8,128)S(1)}, u32[]{:S(2)}, u32[]{:S(2)}) collective-permute-start(f32[2,2,16,128]{3,2,1,0:T(8,128)S(1)} %get-tuple-element.54), channel_id=1, source_target_pairs={{16,0},{32,16},{48,32},{64,48},{80,64},{96,80},{112,96},{128,112},... | collective-permute-start | bytes 98312 | tf_op jit(solution)/shard_map/ppermute | solution.py:49
  44.5 28.4 %collective-permute-start.5 = (f32[3,32,2,128]{3,2,1,0:T(2,128)S(1)}, f32[3,32,2,128]{3,2,1,0:T(2,128)S(1)}, u32[]{:S(2)}, u32[]{:S(2)}) collective-permute-start(f32[3,32,2,128]{3,2,1,0:T(2,128)S(1)} %get-tuple-element.33), channel_id=1, source_target_pairs={{0,1},{1,2},{2,3},{3,4},{4,5},{5,6},{6,7},{7,8},{8,9},{9,10},{10,1... | collective-permute-start | bytes 294920 | tf_op jit(solution)/shard_map/ppermute | solution.py:40
  44.6 28.3 %collective-permute-start.6 = (f32[3,32,2,128]{3,2,1,0:T(2,128)S(1)}, f32[3,32,2,128]{3,2,1,0:T(2,128)S(1)}, u32[]{:S(2)}, u32[]{:S(2)}) collective-permute-start(f32[3,32,2,128]{3,2,1,0:T(2,128)S(1)} %get-tuple-element.34), channel_id=1, source_target_pairs={{1,0},{2,1},{3,2},{4,3},{5,4},{6,5},{7,6},{8,7},{9,8},{10,9},{11,1... | collective-permute-start | bytes 294920 | tf_op jit(solution)/shard_map/ppermute | solution.py:43
  48.2 24.7 %collective-permute-start.4 = (f32[3,2,16,128]{3,2,1,0:T(8,128)S(1)}, f32[3,2,16,128]{3,2,1,0:T(8,128)S(1)}, u32[]{:S(2)}, u32[]{:S(2)}) collective-permute-start(f32[3,2,16,128]{3,2,1,0:T(8,128)S(1)} %get-tuple-element.31), channel_id=1, source_target_pairs={{0,16},{16,32},{32,48},{48,64},{64,80},{80,96},{96,112},{112,128},... | collective-permute-start | bytes 147464 | tf_op jit(solution)/shard_map/ppermute | solution.py:46
  53.9 19.0 %collective-permute-start.7 = (f32[3,2,16,128]{3,2,1,0:T(8,128)S(1)}, f32[3,2,16,128]{3,2,1,0:T(8,128)S(1)}, u32[]{:S(2)}, u32[]{:S(2)}) collective-permute-start(f32[3,2,16,128]{3,2,1,0:T(8,128)S(1)} %get-tuple-element.32), channel_id=1, source_target_pairs={{16,0},{32,16},{48,32},{64,48},{80,64},{96,80},{112,96},{128,112},... | collective-permute-start | bytes 147464 | tf_op jit(solution)/shard_map/ppermute | solution.py:49
  67.1 20.1 %all-to-all-start.2 = ((f32[16,2,2,16,128]{4,3,2,1,0:T(8,128)}), f32[16,2,2,16,128]{4,3,2,1,0:T(8,128)S(1)}, u32[]{:S(2)}, u32[]{:S(2)}) async-start(f32[16,2,2,16,128]{4,3,2,1,0:T(8,128)} %constant_dynamic-update-slice_fusion.16), calls=%async_computation.2 | async-start | bytes 1048576 | tf_op jit(solution)/shard_map/all_to_all | solution.py:65
  79.6 13.2 %copy-start.3 = (s32[32]{0:T(128)S(1)}, s32[32]{0:T(128)}, u32[]{:S(2)}) copy-start(s32[32]{0:T(128)} %param.9) | copy-start | bytes 388
  87.2 25.7 %all-to-all-start = ((f32[16,3,2,16,128]{4,3,2,1,0:T(8,128)}), f32[16,3,2,16,128]{4,3,2,1,0:T(8,128)S(1)}, u32[]{:S(2)}, u32[]{:S(2)}) async-start(f32[16,3,2,16,128]{4,3,2,1,0:T(8,128)} %constant_dynamic-update-slice_fusion), calls=%async_computation | async-start | bytes 1572864 | tf_op jit(solution)/shard_map/all_to_all | solution.py:65
  112.9 20.3 %all-to-all-start.3 = ((f32[2,2,256,128]{3,1,0,2:T(2,128)}), f32[2,2,256,128]{3,1,0,2:T(2,128)S(1)}, u32[]{:S(2)}, u32[]{:S(2)}) async-start(f32[2,2,256,128]{3,1,0,2:T(2,128)} %copy.50), calls=%async_computation.3 | async-start | bytes 1048576 | tf_op jit(solution)/shard_map/all_to_all | solution.py:77
  133.2 41.4 %all-to-all-start.1 = ((f32[3,2,256,128]{3,1,0,2:T(2,128)}), f32[3,2,256,128]{3,1,0,2:T(2,128)S(1)}, u32[]{:S(2)}, u32[]{:S(2)}) async-start(f32[3,2,256,128]{3,1,0,2:T(2,128)} %copy.46), calls=%async_computation.1 | async-start | bytes 1572864 | tf_op jit(solution)/shard_map/all_to_all | solution.py:77
  137.1 20.4 %collective-permute-start.25 = (f32[2,32,2,128]{3,2,1,0:T(2,128)S(1)}, f32[2,32,2,128]{3,2,1,0:T(2,128)S(1)}, u32[]{:S(2)}, u32[]{:S(2)}) collective-permute-start(f32[2,32,2,128]{3,2,1,0:T(2,128)S(1)} %get-tuple-element.49), channel_id=1, source_target_pairs={{0,1},{1,2},{2,3},{3,4},{4,5},{5,6},{6,7},{7,8},{8,9},{9,10},{10,1... | collective-permute-start | bytes 196616 | tf_op jit(solution)/shard_map/ppermute | solution.py:40
  138.5 18.9 %collective-permute-start.26 = (f32[2,32,2,128]{3,2,1,0:T(2,128)S(1)}, f32[2,32,2,128]{3,2,1,0:T(2,128)S(1)}, u32[]{:S(2)}, u32[]{:S(2)}) collective-permute-start(f32[2,32,2,128]{3,2,1,0:T(2,128)S(1)} %get-tuple-element.50), channel_id=1, source_target_pairs={{1,0},{2,1},{3,2},{4,3},{5,4},{6,5},{7,6},{8,7},{9,8},{10,9},{11,1... | collective-permute-start | bytes 196616 | tf_op jit(solution)/shard_map/ppermute | solution.py:43
  140.7 11.7 %collective-permute-start.24 = (f32[2,2,16,128]{3,2,1,0:T(8,128)S(1)}, f32[2,2,16,128]{3,2,1,0:T(8,128)S(1)}, u32[]{:S(2)}, u32[]{:S(2)}) collective-permute-start(f32[2,2,16,128]{3,2,1,0:T(8,128)S(1)} %get-tuple-element.47), channel_id=1, source_target_pairs={{0,16},{16,32},{32,48},{48,64},{64,80},{80,96},{96,112},{112,128},... | collective-permute-start | bytes 98312 | tf_op jit(solution)/shard_map/ppermute | solution.py:46
  150.5 6.9 %collective-permute-start.27 = (f32[2,2,16,128]{3,2,1,0:T(8,128)S(1)}, f32[2,2,16,128]{3,2,1,0:T(8,128)S(1)}, u32[]{:S(2)}, u32[]{:S(2)}) collective-permute-start(f32[2,2,16,128]{3,2,1,0:T(8,128)S(1)} %get-tuple-element.48), channel_id=1, source_target_pairs={{16,0},{32,16},{48,32},{64,48},{80,64},{96,80},{112,96},{128,112},... | collective-permute-start | bytes 98312 | tf_op jit(solution)/shard_map/ppermute | solution.py:49
  158.9 23.1 %collective-permute-start.29 = (f32[2,32,2,128]{3,2,1,0:T(2,128)S(1)}, f32[2,32,2,128]{3,2,1,0:T(2,128)S(1)}, u32[]{:S(2)}, u32[]{:S(2)}) collective-permute-start(f32[2,32,2,128]{3,2,1,0:T(2,128)S(1)} %get-tuple-element.45), channel_id=1, source_target_pairs={{0,1},{1,2},{2,3},{3,4},{4,5},{5,6},{6,7},{7,8},{8,9},{9,10},{10,1... | collective-permute-start | bytes 196616 | tf_op jit(solution)/shard_map/ppermute | solution.py:40
  159.6 27.8 %collective-permute-start.30 = (f32[2,32,2,128]{3,2,1,0:T(2,128)S(1)}, f32[2,32,2,128]{3,2,1,0:T(2,128)S(1)}, u32[]{:S(2)}, u32[]{:S(2)}) collective-permute-start(f32[2,32,2,128]{3,2,1,0:T(2,128)S(1)} %get-tuple-element.46), channel_id=1, source_target_pairs={{1,0},{2,1},{3,2},{4,3},{5,4},{6,5},{7,6},{8,7},{9,8},{10,9},{11,1... | collective-permute-start | bytes 196616 | tf_op jit(solution)/shard_map/ppermute | solution.py:43
  162.5 12.5 %collective-permute-start.28 = (f32[2,2,16,128]{3,2,1,0:T(8,128)S(1)}, f32[2,2,16,128]{3,2,1,0:T(8,128)S(1)}, u32[]{:S(2)}, u32[]{:S(2)}) collective-permute-start(f32[2,2,16,128]{3,2,1,0:T(8,128)S(1)} %get-tuple-element.43), channel_id=1, source_target_pairs={{0,16},{16,32},{32,48},{48,64},{64,80},{80,96},{96,112},{112,128},... | collective-permute-start | bytes 98312 | tf_op jit(solution)/shard_map/ppermute | solution.py:46
  172.7 7.4 %collective-permute-start.31 = (f32[2,2,16,128]{3,2,1,0:T(8,128)S(1)}, f32[2,2,16,128]{3,2,1,0:T(8,128)S(1)}, u32[]{:S(2)}, u32[]{:S(2)}) collective-permute-start(f32[2,2,16,128]{3,2,1,0:T(8,128)S(1)} %get-tuple-element.44), channel_id=1, source_target_pairs={{16,0},{32,16},{48,32},{64,48},{80,64},{96,80},{112,96},{128,112},... | collective-permute-start | bytes 98312 | tf_op jit(solution)/shard_map/ppermute | solution.py:49
  174.9 13.4 %collective-permute-start.10 = (f32[3,32,2,128]{3,2,1,0:T(2,128)S(1)}, f32[3,32,2,128]{3,2,1,0:T(2,128)S(1)}, u32[]{:S(2)}, u32[]{:S(2)}) collective-permute-start(f32[3,32,2,128]{3,2,1,0:T(2,128)S(1)} %get-tuple-element.28), channel_id=1, source_target_pairs={{1,0},{2,1},{3,2},{4,3},{5,4},{6,5},{7,6},{8,7},{9,8},{10,9},{11,1... | collective-permute-start | bytes 294920 | tf_op jit(solution)/shard_map/ppermute | solution.py:43
  175.0 13.3 %collective-permute-start.9 = (f32[3,32,2,128]{3,2,1,0:T(2,128)S(1)}, f32[3,32,2,128]{3,2,1,0:T(2,128)S(1)}, u32[]{:S(2)}, u32[]{:S(2)}) collective-permute-start(f32[3,32,2,128]{3,2,1,0:T(2,128)S(1)} %get-tuple-element.27), channel_id=1, source_target_pairs={{0,1},{1,2},{2,3},{3,4},{4,5},{5,6},{6,7},{7,8},{8,9},{9,10},{10,1... | collective-permute-start | bytes 294920 | tf_op jit(solution)/shard_map/ppermute | solution.py:40
  180.1 7.5 %collective-permute-start.11 = (f32[3,2,16,128]{3,2,1,0:T(8,128)S(1)}, f32[3,2,16,128]{3,2,1,0:T(8,128)S(1)}, u32[]{:S(2)}, u32[]{:S(2)}) collective-permute-start(f32[3,2,16,128]{3,2,1,0:T(8,128)S(1)} %get-tuple-element.26), channel_id=1, source_target_pairs={{16,0},{32,16},{48,32},{64,48},{80,64},{96,80},{112,96},{128,112},... | collective-permute-start | bytes 147464 | tf_op jit(solution)/shard_map/ppermute | solution.py:49
  182.0 6.3 %collective-permute-start.8 = (f32[3,2,16,128]{3,2,1,0:T(8,128)S(1)}, f32[3,2,16,128]{3,2,1,0:T(8,128)S(1)}, u32[]{:S(2)}, u32[]{:S(2)}) collective-permute-start(f32[3,2,16,128]{3,2,1,0:T(8,128)S(1)} %get-tuple-element.25), channel_id=1, source_target_pairs={{0,16},{16,32},{32,48},{48,64},{64,80},{80,96},{96,112},{112,128},... | collective-permute-start | bytes 147464 | tf_op jit(solution)/shard_map/ppermute | solution.py:46
  190.8 16.9 %collective-permute-start.13 = (f32[3,32,2,128]{3,2,1,0:T(2,128)S(1)}, f32[3,32,2,128]{3,2,1,0:T(2,128)S(1)}, u32[]{:S(2)}, u32[]{:S(2)}) collective-permute-start(f32[3,32,2,128]{3,2,1,0:T(2,128)S(1)} %get-tuple-element.23), channel_id=1, source_target_pairs={{0,1},{1,2},{2,3},{3,4},{4,5},{5,6},{6,7},{7,8},{8,9},{9,10},{10,1... | collective-permute-start | bytes 294920 | tf_op jit(solution)/shard_map/ppermute | solution.py:40
  190.9 16.8 %collective-permute-start.14 = (f32[3,32,2,128]{3,2,1,0:T(2,128)S(1)}, f32[3,32,2,128]{3,2,1,0:T(2,128)S(1)}, u32[]{:S(2)}, u32[]{:S(2)}) collective-permute-start(f32[3,32,2,128]{3,2,1,0:T(2,128)S(1)} %get-tuple-element.24), channel_id=1, source_target_pairs={{1,0},{2,1},{3,2},{4,3},{5,4},{6,5},{7,6},{8,7},{9,8},{10,9},{11,1... | collective-permute-start | bytes 294920 | tf_op jit(solution)/shard_map/ppermute | solution.py:43
  194.4 9.5 %collective-permute-start.12 = (f32[3,2,16,128]{3,2,1,0:T(8,128)S(1)}, f32[3,2,16,128]{3,2,1,0:T(8,128)S(1)}, u32[]{:S(2)}, u32[]{:S(2)}) collective-permute-start(f32[3,2,16,128]{3,2,1,0:T(8,128)S(1)} %get-tuple-element.21), channel_id=1, source_target_pairs={{0,16},{16,32},{32,48},{48,64},{64,80},{80,96},{96,112},{112,128},... | collective-permute-start | bytes 147464 | tf_op jit(solution)/shard_map/ppermute | solution.py:46
  200.7 6.9 %collective-permute-start.15 = (f32[3,2,16,128]{3,2,1,0:T(8,128)S(1)}, f32[3,2,16,128]{3,2,1,0:T(8,128)S(1)}, u32[]{:S(2)}, u32[]{:S(2)}) collective-permute-start(f32[3,2,16,128]{3,2,1,0:T(8,128)S(1)} %get-tuple-element.22), channel_id=1, source_target_pairs={{16,0},{32,16},{48,32},{64,48},{80,64},{96,80},{112,96},{128,112},... | collective-permute-start | bytes 147464 | tf_op jit(solution)/shard_map/ppermute | solution.py:49
